TPU v7x, 128 devices: a whole 4x4x4 slice. The times are simulated.
128 devices in a mesh: dp: 32 (over z, x, core), tensor: 4 (over y).
Axes of the slice: x: 4, y: 4, z: 4, core: 2. Of those that a mesh axis runs over, the one named last changes fastest.
Arguments:
- normed_hidden_state: bfloat16 [4, 2048, 8192], P(None, 'dp', 'tensor'), may hold values from -6 to 6
- query_projection_weight: bfloat16 [8192, 4096], P(None, 'tensor'), may hold values from -0.0625 to 0.0625
- adapter_down_maps: bfloat16 [4096, 8192], P('dp', 'tensor'), may hold values from -0.0625 to 0.0625
- adapter_up_maps: bfloat16 [4096, 4096], P('dp', 'tensor'), may hold values from -0.75 to 0.75
- key_value_cache: bfloat16 [2, 2048, 128, 512], P(None, 'dp', None, 'tensor'), may hold values from -82 to 82
- step_key_value: bfloat16 [4, 2, 2048, 512], P(None, None, 'dp', 'tensor'), may hold values from -6 to 6
- cache_valid_length: int32 [2048], P('dp'), may hold values from 1 to 128, as said below
- adapter_per_request: int32 [2048], P('dp'), may hold values from 0 to 63, as said below
- adapter_pool_position: int32 [64], replicated, may hold values from 0 to 63, as said below
Outputs:
- attended: bfloat16 [4, 2048, 4096], P(None, 'dp', 'tensor')
Inputs may be any that keep to these rules, and one draw needn't show every extreme that they name: `adapter_pool_position`: A permutation: every adapter has its own pool position, and position p is held by dp index p // 2. `adapter_per_request`: within each group of 64 consecutive requests, requests whose adapters sit on the same dp index use the same adapter; some dp index serves an adapter to every group. `cache_valid_length`: each group of 64 consecutive requests holds a request with all 128 positions valid.
All inputs are finite; a program needn't handle non-finite values.
Results may differ from a plain program's by a relative error of at most 0.015.
Values may be sent and summed in bfloat16 or wider, within the bound.
No kernel may reach another device: no remote copies, remote signals or barrier semaphores. Data moves between devices by JAX's collectives and lax.ppermute only.
A program may use at most 192 MiB of HBM per device.

v0:
```python
import math
import jax
import jax.numpy as jnp
from jax import lax
from jax.sharding import PartitionSpec as P

HEAD_SIZE = 128
ADAPTER_RANK = 64


def pool_lookup(adapters, adapter_pool_position):
    table = jnp.arange(adapter_pool_position.shape[0], dtype=jnp.int32)
    match = adapters[:, None] == table[None, :]
    return jnp.sum(jnp.where(match, adapter_pool_position[None, :], 0), axis=1)


def adapt_rows(normed_hidden_state, down_map_pages, up_map_pages):
    shrink_local = jnp.einsum(
        "trd,rjd->trj", normed_hidden_state, down_map_pages, preferred_element_type=jnp.float32
    )
    shrink = lax.psum(shrink_local, "tensor").astype(jnp.bfloat16)
    return jnp.einsum("trj,rjh->trh", shrink, up_map_pages, preferred_element_type=jnp.float32)


def attend(query, key_value_cache, step_key_value, cache_valid_length):
    steps = step_key_value.shape[0]
    requests = step_key_value.shape[2]
    length = key_value_cache.shape[2]
    kv_local = key_value_cache.shape[3] // HEAD_SIZE
    group = query.shape[2] // HEAD_SIZE // kv_local
    scale = 1.0 / math.sqrt(HEAD_SIZE)
    grouped = query.reshape(steps, requests, kv_local, group, HEAD_SIZE)
    keys = key_value_cache[0].reshape(requests, length, kv_local, HEAD_SIZE)
    values = key_value_cache[1].reshape(requests, length, kv_local, HEAD_SIZE)
    new_keys = step_key_value[:, 0].reshape(steps, requests, kv_local, HEAD_SIZE)
    new_values = step_key_value[:, 1].reshape(steps, requests, kv_local, HEAD_SIZE)
    cache_scores = (
        jnp.einsum("trkgd,rckd->trkgc", grouped, keys, preferred_element_type=jnp.float32) * scale
    )
    valid = jnp.arange(length, dtype=jnp.int32)[None, :] < cache_valid_length[:, None]
    cache_scores = jnp.where(valid[None, :, None, None, :], cache_scores, -1e30)
    fresh_scores = (
        jnp.einsum("trkgd,srkd->trkgs", grouped, new_keys, preferred_element_type=jnp.float32)
        * scale
    )
    causal = (
        jnp.arange(steps, dtype=jnp.int32)[:, None] >= jnp.arange(steps, dtype=jnp.int32)[None, :]
    )
    fresh_scores = jnp.where(causal[:, None, None, None, :], fresh_scores, -1e30)
    top = jnp.maximum(jnp.max(cache_scores, axis=-1), jnp.max(fresh_scores, axis=-1))
    cache_expo = jnp.exp(cache_scores - top[..., None])
    fresh_expo = jnp.exp(fresh_scores - top[..., None])
    total = jnp.sum(cache_expo, axis=-1) + jnp.sum(fresh_expo, axis=-1)
    mixed = jnp.einsum(
        "trkgc,rckd->trkgd",
        cache_expo.astype(jnp.bfloat16),
        values,
        preferred_element_type=jnp.float32,
    )
    mixed = mixed + jnp.einsum(
        "trkgs,srkd->trkgd",
        fresh_expo.astype(jnp.bfloat16),
        new_values,
        preferred_element_type=jnp.float32,
    )
    attended = mixed / total[..., None]
    return attended.reshape(steps, requests, -1).astype(jnp.bfloat16)


def per_device(
    normed_hidden_state,
    query_projection_weight,
    adapter_down_maps,
    adapter_up_maps,
    key_value_cache,
    step_key_value,
    cache_valid_length,
    adapter_per_request,
    adapter_pool_position,
):
    steps, requests, part_width = normed_hidden_state.shape
    count_rows = steps * requests
    token_rows = normed_hidden_state.reshape(count_rows, part_width)
    heads_width = query_projection_weight.shape[1]
    position = pool_lookup(adapter_per_request, adapter_pool_position)
    base = jnp.dot(
        lax.all_gather(token_rows, "tensor", axis=1, tiled=True),
        query_projection_weight,
        preferred_element_type=jnp.float32,
    )
    down_all, up_all = (
        lax.all_gather(adapter_down_maps, "dp", axis=0, tiled=True),
        lax.all_gather(adapter_up_maps, "dp", axis=0, tiled=True),
    )
    down_map_pages = jnp.take(down_all.reshape(-1, ADAPTER_RANK, part_width), position, axis=0)
    up_map_pages = jnp.take(up_all.reshape(-1, ADAPTER_RANK, heads_width), position, axis=0)
    delta = adapt_rows(normed_hidden_state, down_map_pages, up_map_pages)
    query = (base.reshape(steps, requests, heads_width) + delta).astype(jnp.bfloat16)
    return attend(query, key_value_cache, step_key_value, cache_valid_length)


def solution(mesh):
    return jax.shard_map(
        per_device,
        mesh=mesh,
        in_specs=(
            P(None, "dp", "tensor"),
            P(None, "tensor"),
            P("dp", "tensor"),
            P("dp", "tensor"),
            P(None, "dp", None, "tensor"),
            P(None, None, "dp", "tensor"),
            P("dp"),
            P("dp"),
            P(),
        ),
        out_specs=P(None, "dp", "tensor"),
        check_vma=False,
    )
```

profile of v0, /device:TPU:0, one launch (start us, length us, event | category | flops | bytes accessed | tf_op | source)
XLA Modules:
  0.0 252.2 jit_solution(4320837906704978882)
XLA Ops:
  6.5 0.0 all-gather.4.cloned.1.call-start
  6.5 0.7 all-gather.4.cloned.1.call-update
  7.3 0.0 all-gather.6.cloned.1.call-start
  7.3 0.7 all-gather.6.cloned.1.call-update
  8.0 0.0 all-gather.8.cloned.1.call-start
  8.1 0.7 all-gather.8.cloned.1.call-update
  8.8 0.8 select_reduce_fusion
  9.6 0.7 iota_compare_fusion.1
  10.4 0.9 fusion.56
  11.3 48.5 %all-gather.4.cloned.1.call-done = bf16[256,8192]{1,0:T(8,128)(2,1)} async-done(((bf16[256,2048]{1,0:T(8,128)(2,1)}), bf16[256,8192]{1,0:T(8,128)(2,1)}) %all-gather.4.cloned.1.call-update) | async-done | bytes 4194320 | tf_op jit(solution)/shard_map/all_gather | solution.py:87
  59.7 9.6 %fusion.59 = f32[256,1024]{1,0:T(8,128)S(1)} fusion(bf16[256,8192]{1,0:T(8,128)(2,1)} %all-gather.4.cloned.1.call-done, bf16[8192,1024]{1,0:T(8,128)(2,1)} %param.10), kind=kOutput, calls=%fused_computation.58 | convolution fusion | flops 4294967296 | bytes 22020096 | tf_op jit(solution)/shard_map/dot_general | solution.py:86
  69.3 45.8 %all-gather.6.cloned.1.call-done = bf16[4096,1024]{1,0:T(8,128)(2,1)} async-done(((bf16[128,1024]{1,0:T(8,128)(2,1)}), bf16[4096,1024]{1,0:T(8,128)(2,1)}) %all-gather.6.cloned.1.call-update) | async-done | bytes 8388624 | tf_op jit(solution)/shard_map/all_gather | solution.py:93
  115.2 8.9 %gather_fusion = bf16[64,64,1024]{2,1,0:T(8,128)(2,1)} fusion(bf16[64,64,1024]{2,1,0:T(8,128)(2,1)} %bitcast.96, s32[1024]{0:T(1024)S(1)} %pad_clamp_fusion), kind=kCustom, calls=%fused_computation | custom fusion | bytes 16777472 | tf_op jit(solution)/shard_map/jit(_take)/gather | solution.py:96
  124.1 65.6 %all-gather.8.cloned.1.call-done = bf16[4096,2048]{1,0:T(8,128)(2,1)} async-done(((bf16[128,2048]{1,0:T(8,128)(2,1)}), bf16[4096,2048]{1,0:T(8,128)(2,1)}) %all-gather.8.cloned.1.call-update) | async-done | bytes 16777232 | tf_op jit(solution)/shard_map/all_gather | solution.py:92
  189.7 0.0 copy-start
  189.7 13.4 %gather_fusion.1 = bf16[64,64,2048]{2,1,0:T(8,128)(2,1)} fusion(bf16[64,64,2048]{2,1,0:T(8,128)(2,1)} %bitcast.95, s32[1024]{0:T(1024)S(1)} %pad_clamp_fusion), kind=kCustom, calls=%fused_computation.1 | custom fusion | bytes 33554688 | tf_op jit(solution)/shard_map/jit(_take)/gather | solution.py:95
  203.1 0.0 copy-done
  203.1 8.1 %fusion.37 = f32[4,64,64]{2,0,1:T(4,128)S(1)} fusion(bf16[64,64,2048]{2,1,0:T(8,128)(2,1)} %gather_fusion.1, pred[64]{0:T(512)(128)(4,1)S(1)} %compare_and_fusion, bf16[4,64,2048]{2,1,0:T(8,128)(2,1)S(1)} %copy-done), kind=kOutput, calls=%fused_computation.27 | convolution fusion | flops 75497472 | bytes 17891392 | tf_op jit(solution)/shard_map/trd,rjd->trj/dot_general | solution.py:18
  211.2 18.5 %psum.7 = bf16[4,64,64]{2,0,1:T(4,128)(2,1)S(1)} all-reduce(f32[4,64,64]{2,0,1:T(4,128)S(1)} %fusion.37), channel_id=1, replica_groups=mesh['dp'=32,'tensor'=4] {'tensor'}, use_global_device_ids=true, to_apply=%region_1.2 | all-reduce | flops 16384 | bytes 98304 | tf_op jit(solution)/shard_map/psum | solution.py:21
  229.8 4.9 %fusion.27 = bf16[4,64,1024]{2,0,1:T(4,128)(2,1)S(1)} fusion(bf16[64,64,1024]{2,1,0:T(8,128)(2,1)} %gather_fusion, pred[64]{0:T(512)(128)(4,1)S(1)} %compare_and_fusion, f32[4,64,1024]{2,1,0:T(8,128)S(1)} %bitcast.98, bf16[4,64,64]{2,0,1:T(4,128)(2,1)S(1)} %psum.7), kind=kOutput, calls=%fused_computation.22 | convolution fusion | flops 38273024 | bytes 9994304 | tf_op jit(solution)/shard_map/trj,rjh->trh/dot_general | solution.py:22
  234.7 0.2 reshape.139
  234.9 2.4 fusion.58
  237.3 2.9 %fusion.57 = (f32[4,64,8]{2,0,1:T(4,128)S(1)}, f32[4,64,1,8,128]{4,3,0,1,2:T(8,128)S(1)}) fusion(bf16[4,64,8,128]{3,2,0,1:T(8,128)(2,1)S(1)} %reshape.139, bf16[2,64,128,128]{3,2,1,0:T(8,128)(2,1)} %param.13, pred[64,128]{1,0:T(8,128)(4,1)S(1)} %iota_compare_fusion.1), kind=kOutput, calls=%fused_computation.56 | convolution fusion | flops 67893248 | bytes 3686400 | tf_op jit(solution)/shard_map/trkgd,rckd->trkgc/dot_general | solution.py:38
  240.3 0.7 fusion.42
  241.0 2.3 fusion.8
  243.4 0.5 fusion.47
  243.9 0.6 divide_convert_fusion
  244.5 0.1 convert_element_type.23
  244.7 1.0 copy.17
  (6 shorter events, 0.1 us)
Async XLA Ops:
  6.5 53.2 %all-gather.4.cloned.1.call-start = ((), (), s32[]{:S(2)}) async-start(), calls=%async_computation | async-start | bytes 5242880 | tf_op jit(solution)/shard_map/all_gather | solution.py:87
  7.3 107.9 %all-gather.6.cloned.1.call-start = ((), (), s32[]{:S(2)}) async-start(), calls=%async_computation.1 | async-start | bytes 8650752 | tf_op jit(solution)/shard_map/all_gather | solution.py:93
  8.0 181.7 %all-gather.8.cloned.1.call-start = ((), (), s32[]{:S(2)}) async-start(), calls=%async_computation.2 | async-start | bytes 17301504 | tf_op jit(solution)/shard_map/all_gather | solution.py:92
  189.7 13.5 %copy-start = (bf16[4,64,2048]{2,1,0:T(8,128)(2,1)S(1)}, bf16[4,64,2048]{2,1,0:T(8,128)(2,1)}, u32[]{:S(2)}) copy-start(bf16[4,64,2048]{2,1,0:T(8,128)(2,1)} %param.9) | copy-start | bytes 3145732
Sparse Core Ops, SparseCore 0:
  9.0 50.6 all-gather.3
  62.0 53.1 all-gather.5
  117.5 72.1 all-gather.7
where the time goes:
time: 252 us
  waiting for transfers between devices  162 us (64%)
  matrix products  30.9 us (12%)
  local copies, waits for them, and re-layouts  24.5 us (10%)
  blocking collectives  18.5 us (7%)
  between operations  13.2 us (5%)
  other arithmetic  2.9 us (1%)
    all_gather x1, waiting for transfers between devices, per_device(): lax.all_gather(adapter_down_maps, 'dp', axis=0, tiled=True)  65.6 us
    all_gather x1, waiting for transfers between devices, per_device(): lax.all_gather(token_rows, 'tensor', axis=1, tiled=True)  48.5 us
    all_gather x1, waiting for transfers between devices, per_device(): lax.all_gather(adapter_up_maps, 'dp', axis=0, tiled=True)  45.8 us
    psum x1, blocking collectives, adapt_rows(): shrink = lax.psum(shrink_local, 'tensor').astype(jnp.bfloat16)  18.5 us
    gather x1, local copies, waits for them, and re-layouts, per_device(): jnp.take(down_all.reshape(-1, ADAPTER_RANK, part_width), position, axis=0)  13.4 us
    dot_general x1, matrix products, per_device(): jnp.dot(lax.all_gather(token_rows, 'tensor', axis=1, tiled=True), query_p...  9.61 us
    gather x1, local copies, waits for them, and re-layouts, per_device(): jnp.take(up_all.reshape(-1, ADAPTER_RANK, heads_width), position, axis=0)  8.89 us
    dot_general x1, matrix products, adapt_rows(): jnp.einsum('trd,rjd->trj', normed_hidden_state, down_map_pages, preferred...  8.13 us
  transfers between devices with their start and end apart: 3, of which 3 were waited for; matrix products, arithmetic and copies ran while one was open for 8% of the time, Pallas kernels for 0%

commit v1 on v0

--- a/solution.py
+++ b/solution.py
@@ -6,6 +6,28 @@
 
 HEAD_SIZE = 128
 ADAPTER_RANK = 64
+
+
+def in_order(blocks, dim):
+    blocks = jnp.moveaxis(blocks, 0, dim)
+    lengths = blocks.shape
+    return blocks.reshape(*lengths[:dim], lengths[dim] * lengths[dim + 1], *lengths[dim + 2 :])
+
+
+def collect(x, axis, dim):
+    count = lax.axis_size(axis)
+    pairs = [(i, (i + 1) % count) for i in range(count)]
+    back = [(b, a) for a, b in pairs]
+    lower, upper = ([], [])
+    for step in range(count - 1):
+        if step % 2 == 0:
+            lower.append(lax.ppermute(lower[-1] if lower else x, axis, pairs))
+        else:
+            upper.append(lax.ppermute(upper[-1] if upper else x, axis, back))
+    tiles = jnp.stack([*lower[::-1], x, *upper])
+    shift = lax.axis_index(axis) - len(lower)
+    tiles = tiles[(jnp.arange(count) - shift) % count]
+    return in_order(tiles, dim)
 
 
 def pool_lookup(adapters, adapter_pool_position):
@@ -84,7 +106,7 @@
     heads_width = query_projection_weight.shape[1]
     position = pool_lookup(adapter_per_request, adapter_pool_position)
     base = jnp.dot(
-        lax.all_gather(token_rows, "tensor", axis=1, tiled=True),
+        collect(token_rows, "tensor", 1),
         query_projection_weight,
         preferred_element_type=jnp.float32,
     )

time: 252 us -> 208 us (0.83)
  waiting for transfers between devices: 162 us -> 94.1 us
  local copies, waits for them, and re-layouts: 24.5 us -> 44.8 us
  matrix products: 30.9 us -> 27.1 us
  starting transfers between devices: 0.08 us -> 3.65 us
  other arithmetic: 2.9 us -> 6.26 us
    all_gather x1 -> x0, waiting for transfers between devices: 48.5 us -> none  [per_device(): lax.all_gather(token_rows, 'tensor', axis=1, tiled=True)]
    all_gather x1, waiting for transfers between devices: 45.8 us -> 0.01 us  [per_device(): lax.all_gather(adapter_up_maps, 'dp', axis=0, tiled=True)]
    ppermute x0 -> x3, waiting for transfers between devices: none -> 45.8 us  [the longest x2 45.8 us: collect(): lower.append(lax.ppermute(lower[-1] if lower else x, axis, pairs))]
    all_gather x1, waiting for transfers between devices: 65.6 us -> 46.8 us  [per_device(): lax.all_gather(adapter_down_maps, 'dp', axis=0, tiled=True)]
    dot_general x0 -> x1, local copies, waits for them, and re-layouts: none -> 7.8 us  [per_device(): jnp.dot(collect(token_rows, 'tensor', 1), query_projection_weight, prefer...]
    transpose x0 -> x1, local copies, waits for them, and re-layouts: none -> 7.37 us  [in_order(): blocks = jnp.moveaxis(blocks, 0, dim)]
    gather x0 -> x1, local copies, waits for them, and re-layouts: none -> 5.06 us  [collect(): tiles = tiles[(jnp.arange(count) - shift) % count]]
    ppermute x0 -> x3, starting transfers between devices: none -> 3.61 us  [the longest x2 2.06 us: collect(): lower.append(lax.ppermute(lower[-1] if lower else x, axis, pairs))]
  transfers between devices with their start and end apart: 3 -> 5, of which waited for: 3 -> 3; matrix products, arithmetic and copies ran while one was open for 8% -> 17% of each run, Pallas kernels for 0% -> 0%
where the time goes in v1:
time: 208 us
  waiting for transfers between devices  94.1 us (45%)
  local copies, waits for them, and re-layouts  44.8 us (22%)
  matrix products  27.1 us (13%)
  blocking collectives  18.5 us (9%)
  between operations  13.5 us (6%)
  other arithmetic  6.26 us (3%)
  starting transfers between devices  3.65 us (2%)
    all_gather x1, waiting for transfers between devices, per_device(): lax.all_gather(adapter_down_maps, 'dp', axis=0, tiled=True)  46.8 us
    ppermute x2, waiting for transfers between devices, collect(): lower.append(lax.ppermute(lower[-1] if lower else x, axis, pairs))  45.8 us
    psum x1, blocking collectives, adapt_rows(): shrink = lax.psum(shrink_local, 'tensor').astype(jnp.bfloat16)  18.5 us
    gather x1, local copies, waits for them, and re-layouts, per_device(): jnp.take(down_all.reshape(-1, ADAPTER_RANK, part_width), position, axis=0)  13.4 us
    gather x1, local copies, waits for them, and re-layouts, per_device(): jnp.take(up_all.reshape(-1, ADAPTER_RANK, heads_width), position, axis=0)  9.02 us
    dot_general x1, matrix products, per_device(): jnp.dot(collect(token_rows, 'tensor', 1), query_projection_weight, prefer...  8.91 us
    dot_general x1, matrix products, adapt_rows(): jnp.einsum('trd,rjd->trj', normed_hidden_state, down_map_pages, preferred...  8.13 us
    dot_general x1, local copies, waits for them, and re-layouts, per_device(): jnp.dot(collect(token_rows, 'tensor', 1), query_projection_weight, prefer...  7.8 us
  transfers between devices with their start and end apart: 5, of which 3 were waited for; matrix products, arithmetic and copies ran while one was open for 17% of the time, Pallas kernels for 0%

profile of v1, /device:TPU:0, one launch (start us, length us, event | category | flops | bytes accessed | tf_op | source)
XLA Modules:
  0.0 207.9 jit_solution(9372038206658024775)
XLA Ops:
  6.5 0.0 all-gather.3.cloned.1.call-start
  6.5 0.7 all-gather.3.cloned.1.call-update
  7.3 0.0 all-gather.5.cloned.1.call-start
  7.3 0.7 all-gather.5.cloned.1.call-update
  8.0 1.8 collective-permute-start
  9.8 1.5 collective-permute-start.2
  11.3 0.9 select_reduce_fusion
  12.2 22.4 %collective-permute-done = bf16[256,2048]{1,0:T(8,128)(2,1)S(1)} collective-permute-done((bf16[256,2048]{1,0:T(8,128)(2,1)}, bf16[256,2048]{1,0:T(8,128)(2,1)S(1)}, u32[]{:S(2)}, u32[]{:S(2)}) %collective-permute-start) | collective-permute-done | bytes 1048608 | tf_op jit(solution)/shard_map/ppermute | solution.py:24
  34.6 0.3 collective-permute-start.1
  34.9 0.7 iota_compare_fusion.1
  35.7 0.9 fusion.59
  36.6 0.0 collective-permute-done.2
  36.6 23.4 %collective-permute-done.1 = bf16[256,2048]{1,0:T(8,128)(2,1)S(1)} collective-permute-done((bf16[256,2048]{1,0:T(8,128)(2,1)S(1)}, bf16[256,2048]{1,0:T(8,128)(2,1)S(1)}, u32[]{:S(2)}, u32[]{:S(2)}) %collective-permute-start.1) | collective-permute-done | bytes 1048608 | tf_op jit(solution)/shard_map/ppermute | solution.py:24
  60.0 3.3 %pad_maximum_fusion = bf16[4,256,2048]{2,1,0:T(8,128)(2,1)} fusion(bf16[1,256,2048]{2,1,0:T(8,128)(2,1)S(1)} %bitcast.124, bf16[1,256,2048]{2,1,0:T(8,128)(2,1)} %bitcast.122, bf16[1,256,2048]{2,1,0:T(8,128)(2,1)S(1)} %bitcast.123, bf16[1,256,2048]{2,1,0:T(8,128)(2,1)S(1)} %bitcast.125), kind=kLoop, calls=%fused_computation.12 | loop fusion | flops 6291456 | bytes 8388608 | tf_op jit(solution)/shard_map/stack | solution.py:27
  63.3 5.1 %gather_fusion = bf16[4,256,2048]{2,1,0:T(8,128)(2,1)} fusion(bf16[4,256,2048]{2,1,0:T(8,128)(2,1)} %pad_maximum_fusion, s32[1024]{0:T(1024)S(1)} %pad_clamp_fusion.1), kind=kCustom, calls=%fused_computation | custom fusion | bytes 8388624 | tf_op jit(solution)/shard_map/gather | solution.py:29
  68.4 7.4 %copy.17 = bf16[256,4,2048]{2,1,0:T(4,128)(2,1)} copy(bf16[256,4,2048]{2,0,1:T(8,128)(2,1)} %bitcast.116) | data formatting | bytes 8388608 | tf_op jit(solution)/shard_map/transpose | solution.py:12
  75.8 7.8 %dot_general.23 = bf16[4,64,8192]{2,1,0:T(8,128)(2,1)} reshape(bf16[256,4,2048]{2,1,0:T(4,128)(2,1)} %copy.17) | data formatting | bytes 8388608 | tf_op jit(solution)/shard_map/dot_general | solution.py:108
  83.6 0.0 all-gather.3.cloned.1.call-done
  83.6 9.0 %gather_fusion.1 = bf16[64,64,1024]{2,1,0:T(8,128)(2,1)} fusion(bf16[64,64,1024]{2,1,0:T(8,128)(2,1)} %bitcast.117, s32[1024]{0:T(1024)S(1)} %pad_clamp_fusion), kind=kCustom, calls=%fused_computation.1 | custom fusion | bytes 16777472 | tf_op jit(solution)/shard_map/jit(_take)/gather | solution.py:118
  92.6 46.8 %all-gather.5.cloned.1.call-done = bf16[4096,2048]{1,0:T(8,128)(2,1)} async-done(((bf16[128,2048]{1,0:T(8,128)(2,1)}), bf16[4096,2048]{1,0:T(8,128)(2,1)}) %all-gather.5.cloned.1.call-update) | async-done | bytes 16777232 | tf_op jit(solution)/shard_map/all_gather | solution.py:114
  139.4 0.0 copy-start.2
  139.4 13.4 %gather_fusion.2 = bf16[64,64,2048]{2,1,0:T(8,128)(2,1)} fusion(bf16[64,64,2048]{2,1,0:T(8,128)(2,1)} %bitcast.115, s32[1024]{0:T(1024)S(1)} %pad_clamp_fusion), kind=kCustom, calls=%fused_computation.2 | custom fusion | bytes 33554688 | tf_op jit(solution)/shard_map/jit(_take)/gather | solution.py:117
  152.9 0.0 copy-done.2
  152.9 8.1 %fusion.36 = f32[4,64,64]{2,0,1:T(4,128)S(1)} fusion(bf16[64,64,2048]{2,1,0:T(8,128)(2,1)} %gather_fusion.2, pred[64]{0:T(512)(128)(4,1)S(1)} %compare_and_fusion, bf16[4,64,2048]{2,1,0:T(8,128)(2,1)S(1)} %copy-done.2), kind=kOutput, calls=%fused_computation.30 | convolution fusion | flops 75497472 | bytes 17891392 | tf_op jit(solution)/shard_map/trd,rjd->trj/dot_general | solution.py:40
  161.0 18.5 %psum.7 = bf16[4,64,64]{2,0,1:T(4,128)(2,1)S(1)} all-reduce(f32[4,64,64]{2,0,1:T(4,128)S(1)} %fusion.36), channel_id=1, replica_groups=mesh['dp'=32,'tensor'=4] {'tensor'}, use_global_device_ids=true, to_apply=%region_1.2 | all-reduce | flops 16384 | bytes 98304 | tf_op jit(solution)/shard_map/psum | solution.py:43
  179.6 0.0 copy-start
  179.6 4.9 %fusion.6 = f32[64,1024,4]{1,2,0:T(4,128)S(1)} fusion(bf16[64,64,1024]{2,1,0:T(8,128)(2,1)} %gather_fusion.1, pred[64]{0:T(512)(128)(4,1)S(1)} %compare_and_fusion, bf16[4,64,64]{2,0,1:T(4,128)(2,1)S(1)} %psum.7), kind=kOutput, calls=%fused_computation.9 | convolution fusion | flops 37748736 | bytes 9470016 | tf_op jit(solution)/shard_map/trj,rjh->trh/dot_general | solution.py:44
  184.5 0.0 copy-done
  184.5 0.0 copy-start.1
  184.5 8.9 %fusion.26 = bf16[4,64,1024]{2,1,0:T(8,128)(2,1)S(1)} fusion(bf16[4,64,8192]{2,1,0:T(8,128)(2,1)S(1)} %copy-done, bf16[8192,1024]{1,0:T(8,128)(2,1)} %param.10, f32[64,1024,4]{1,2,0:T(4,128)S(1)} %fusion.6), kind=kOutput, calls=%fused_computation.25 | convolution fusion | flops 4295491584 | bytes 22544384 | tf_op jit(solution)/shard_map/dot_general | solution.py:108
  193.4 0.1 copy.31
  193.5 2.5 %fusion.61 = (f32[4,64,8]{2,0,1:T(4,128)S(1)}, f32[4,64,1,8,4]{3,4,0,1,2:T(4,128)S(1)}) fusion(bf16[4,1,64,128]{3,2,1,0:T(8,128)(2,1)S(1)} %get-tuple-element.6, pred[4,4]{1,0:T(4,128)(4,1)S(1)} %iota_compare_fusion.2, bf16[4,64,8,128]{3,2,1,0:T(8,128)(2,1)S(1)} %bitcast.118), kind=kOutput, calls=%fused_computation.69 | convolution fusion | flops 2119680 | bytes 630800 | tf_op jit(solution)/shard_map/trkgd,srkd->trkgs/dot_general | solution.py:65
  196.0 0.0 copy-done.1
  196.0 1.3 fusion.60
  197.4 0.7 fusion.41
  198.1 0.7 fusion.10
  198.9 0.5 fusion.48
  199.4 0.6 divide_convert_fusion
  200.0 0.1 convert_element_type.23
  200.1 1.0 copy.23
  (8 shorter events, 0.1 us)
Async XLA Ops:
  6.5 77.0 %all-gather.3.cloned.1.call-start = ((), (), s32[]{:S(2)}) async-start(), calls=%async_computation | async-start | bytes 8650752 | tf_op jit(solution)/shard_map/all_gather | solution.py:115
  7.3 132.2 %all-gather.5.cloned.1.call-start = ((), (), s32[]{:S(2)}) async-start(), calls=%async_computation.1 | async-start | bytes 17301504 | tf_op jit(solution)/shard_map/all_gather | solution.py:114
  8.0 26.6 %collective-permute-start = (bf16[256,2048]{1,0:T(8,128)(2,1)}, bf16[256,2048]{1,0:T(8,128)(2,1)S(1)}, u32[]{:S(2)}, u32[]{:S(2)}) collective-permute-start(bf16[256,2048]{1,0:T(8,128)(2,1)} %bitcast.120), channel_id=1, source_target_pairs={{0,1},{1,2},{2,3},{3,0},{4,5},{5,6},{6,7},{7,4},{8,9},{9,10},{10,1... | collective-permute-start | bytes 3145736 | tf_op jit(solution)/shard_map/ppermute | solution.py:24
  9.8 26.8 %collective-permute-start.2 = (bf16[256,2048]{1,0:T(8,128)(2,1)}, bf16[256,2048]{1,0:T(8,128)(2,1)S(1)}, u32[]{:S(2)}, u32[]{:S(2)}) collective-permute-start(bf16[256,2048]{1,0:T(8,128)(2,1)} %bitcast.121), channel_id=1, source_target_pairs={{1,0},{2,1},{3,2},{0,3},{5,4},{6,5},{7,6},{4,7},{9,8},{10,9},{11,1... | collective-permute-start | bytes 3145736 | tf_op jit(solution)/shard_map/ppermute | solution.py:26
  34.6 25.4 %collective-permute-start.1 = (bf16[256,2048]{1,0:T(8,128)(2,1)S(1)}, bf16[256,2048]{1,0:T(8,128)(2,1)S(1)}, u32[]{:S(2)}, u32[]{:S(2)}) collective-permute-start(bf16[256,2048]{1,0:T(8,128)(2,1)S(1)} %collective-permute-done), channel_id=1, source_target_pairs={{0,1},{1,2},{2,3},{3,0},{4,5},{5,6},{6,7},{7,4},{8,9},{9,10},{10,1... | collective-permute-start | bytes 3145736 | tf_op jit(solution)/shard_map/ppermute | solution.py:24
  139.4 13.5 %copy-start.2 = (bf16[4,64,2048]{2,1,0:T(8,128)(2,1)S(1)}, bf16[4,64,2048]{2,1,0:T(8,128)(2,1)}, u32[]{:S(2)}) copy-start(bf16[4,64,2048]{2,1,0:T(8,128)(2,1)} %param.9) | copy-start | bytes 3145732
  179.6 4.9 %copy-start = (bf16[4,64,8192]{2,1,0:T(8,128)(2,1)S(1)}, bf16[4,64,8192]{2,1,0:T(8,128)(2,1)}, u32[]{:S(2)}) copy-start(bf16[4,64,8192]{2,1,0:T(8,128)(2,1)} %dot_general.23) | copy-start | bytes 12582916
  184.5 11.5 %copy-start.1 = (bf16[2,64,128,128]{3,2,1,0:T(8,128)(2,1)S(1)}, bf16[2,64,128,128]{3,2,1,0:T(8,128)(2,1)}, u32[]{:S(2)}) copy-start(bf16[2,64,128,128]{3,2,1,0:T(8,128)(2,1)} %param.13) | copy-start | bytes 12582916
Sparse Core Ops, SparseCore 0:
  9.6 55.3 all-gather.2
  67.2 72.1 all-gather.4
